TPU v7x, 512 devices: a whole 4x4x16 slice. The times are simulated.
512 devices in a mesh: seq: 128 (over y, z, core), head: 4 (over x).
Axes of the slice: x: 4, y: 4, z: 16, core: 2. Of those that a mesh axis runs over, the one named last changes fastest.
Arguments:
- tokens: bfloat16 [64, 4, 1024], P('head'), may hold values from -6 to 6
- cache_keys: bfloat16 [64, 4096, 512], P(None, 'seq', 'head'), may hold values from -70 to 70
- cache_values: bfloat16 [64, 4096, 512], P(None, 'seq', 'head'), may hold values from -6 to 6
- held_states: bfloat16 [64, 512, 1024], P(None, 'seq'), may hold values from -6 to 6
- recompute_pos: int32 [64, 512], P(None, 'seq'), may hold values from 0 to 4095, as said below
- cache_len: int32 [64], replicated, may hold values from 1 to 4096
- new_prompt: int32 [64], replicated, may hold values 0 or 1
- w_qkv: bfloat16 [3, 1024, 512], P(None, None, 'head'), may hold values from -0.1875 to 0.1875
- qkv_bias: float32 [3, 512], P(None, 'head'), may hold values from -3 to 3
- w_out: bfloat16 [512, 1024], P('head'), may hold values from -1.5 to 1.5
- out_bias: float32 [1024], replicated, may hold values from -3 to 3
- attn_gain: float32 [1024], replicated, may hold values from 0.1 to 1.9
- attn_shift: float32 [1024], replicated, may hold values from -3 to 3
- w_up: bfloat16 [1024, 2048], P(None, 'head'), may hold values from -0.1875 to 0.1875
- up_bias: float32 [2048], P('head'), may hold values from -3 to 3
- w_down: bfloat16 [2048, 1024], P('head'), may hold values from -0.125 to 0.125
- down_bias: float32 [1024], replicated, may hold values from -3 to 3
- ffn_gain: float32 [1024], replicated, may hold values from 0.1 to 1.9
- ffn_shift: float32 [1024], replicated, may hold values from -3 to 3
Outputs:
- layer_out: bfloat16 [64, 4, 1024], P('head')
Inputs may be any that keep to these rules, and one draw needn't show every extreme that they name: `recompute_pos`: columns s * 4 to (s + 1) * 4 - 1 of a row hold distinct positions from s * 32 to (s + 1) * 32 - 1.
All inputs are finite; a program needn't handle non-finite values.
Results may differ from a plain program's by a relative error of at most 0.011.
Values may be sent and summed in bfloat16 or wider, within the bound.
No kernel may reach another device: no remote copies, remote signals or barrier semaphores. Data moves between devices by JAX's collectives and lax.ppermute only.
A program may use at most 192 MiB of HBM per device.

v0:
```python
import jax
import jax.numpy as jnp
from jax import lax
from jax.sharding import PartitionSpec as P

HDIM = 64
NEG = -1e30
EPS = 1e-05


def layer_norm(values, norm_gain, norm_bias):
    center = jnp.mean(values, axis=-1, keepdims=True)
    spread = values - center
    second = jnp.mean(spread * spread, axis=-1, keepdims=True)
    return spread * lax.rsqrt(second + EPS) * norm_gain + norm_bias


def merge_pair(first_part, second_part):
    first_max, first_sum, first_out = first_part
    second_max, second_sum, second_out = second_part
    joint_max = jnp.maximum(first_max, second_max)
    first_scale = jnp.exp(first_max - joint_max)
    second_scale = jnp.exp(second_max - joint_max)
    return (
        joint_max,
        first_sum * first_scale + second_sum * second_scale,
        first_out * first_scale[..., None] + second_out * second_scale[..., None],
    )


def partial_attention(queries, keys_here, values_here, visible):
    scores = jnp.einsum(
        "rthe,rphe->rthp", queries, keys_here, preferred_element_type=jnp.float32
    ) * HDIM ** (-0.5)
    highest = jnp.max(jnp.where(visible, scores, NEG), axis=-1)
    weights = jnp.exp(jnp.where(visible, scores - highest[..., None], NEG)).astype(jnp.bfloat16)
    totals = jnp.sum(weights.astype(jnp.float32), axis=-1)
    blended = jnp.einsum(
        "rthp,rphe->rthe", weights, values_here, preferred_element_type=jnp.float32
    )
    return (highest, totals, blended)


def seq_merge(block_max, block_sum, block_out):
    n_seq = lax.axis_size("seq")
    head_shape = block_out.shape
    lanes = head_shape[-2] * head_shape[-1]
    rows = block_out.size // lanes
    stat_rows = block_max.size // lanes
    out2 = block_out.reshape(rows, lanes)
    top = block_max.reshape(stat_rows, lanes)
    total = block_sum.reshape(stat_rows, lanes)
    width = head_shape[-1]
    step = 1
    while step < n_seq:
        pairs = [(i, i ^ step) for i in range(n_seq)]
        packed = jnp.concatenate([out2, top, total], axis=0)
        other = lax.ppermute(packed, "seq", pairs)
        o_out = other[:rows]
        o_top = other[rows : rows + stat_rows]
        o_total = other[rows + stat_rows :]
        joint = jnp.maximum(top, o_top)
        mine = jnp.exp(top - joint)
        theirs = jnp.exp(o_top - joint)
        total = total * mine + o_total * theirs
        mine_rows = jnp.repeat(mine.reshape(rows, lanes // width), width, axis=1)
        theirs_rows = jnp.repeat(theirs.reshape(rows, lanes // width), width, axis=1)
        out2 = out2 * mine_rows + o_out * theirs_rows
        top = joint
        step *= 2
    return (top.reshape(block_max.shape), total.reshape(block_sum.shape), out2.reshape(head_shape))


def on_device(
    tokens,
    cache_keys,
    cache_values,
    held_states,
    recompute_pos,
    cache_len,
    new_prompt,
    w_qkv,
    qkv_bias,
    w_out,
    out_bias,
    attn_gain,
    attn_shift,
    w_up,
    up_bias,
    w_down,
    down_bias,
    ffn_gain,
    ffn_shift,
):
    local_width = w_qkv.shape[2]
    local_heads = local_width // HDIM
    requests = cache_keys.shape[0]
    block_len = cache_keys.shape[1]
    own_rows = tokens.shape[0]
    steps_count = tokens.shape[1]
    block_rows = lax.all_gather(tokens, "head", axis=0, tiled=True)
    triple = (
        jnp.einsum("rtd,kdc->rtkc", block_rows, w_qkv, preferred_element_type=jnp.float32)
        + qkv_bias
    )
    triple = triple.astype(jnp.bfloat16).reshape(
        block_rows.shape[0], block_rows.shape[1], 3 * local_width
    )
    gathered = jnp.concatenate([triple, block_rows], axis=2)
    head_shape = (requests, steps_count, local_heads, HDIM)
    queries = gathered[:, :, :local_width].reshape(head_shape)
    new_keys = gathered[:, :, local_width : 2 * local_width].reshape(head_shape)
    new_values = gathered[:, :, 2 * local_width : 3 * local_width].reshape(head_shape)
    fresh_keys = (
        jnp.einsum("rjd,dc->rjc", held_states, w_qkv[1], preferred_element_type=jnp.float32)
        + qkv_bias[1]
    ).astype(jnp.bfloat16)
    offset_pos = lax.axis_index("seq") * block_len
    positions = jnp.arange(block_len, dtype=jnp.int32)
    matches = (recompute_pos - offset_pos)[:, :, None] == positions[None, None, :]
    placed = jnp.einsum(
        "rjp,rjc->rpc", matches.astype(jnp.bfloat16), fresh_keys, preferred_element_type=jnp.float32
    ).astype(jnp.bfloat16)
    replaced = jnp.any(matches, axis=1)
    keys_here = jnp.where(replaced[:, :, None], placed, cache_keys).reshape(
        requests, block_len, local_heads, HDIM
    )
    values_here = cache_values.reshape(requests, block_len, local_heads, HDIM)
    visible = ((offset_pos + positions)[None, :] < cache_len[:, None]) & (new_prompt[:, None] == 0)
    block_max, block_sum, block_out = partial_attention(
        queries, keys_here, values_here, visible[:, None, None, :]
    )
    cache_max, cache_sum, cache_out = seq_merge(block_max, block_sum, block_out)
    order_t = jnp.arange(steps_count, dtype=jnp.int32)
    causal = (order_t[:, None] >= order_t[None, :])[None, :, None, :]
    new_max, new_sum, new_out = partial_attention(queries, new_keys, new_values, causal)
    joint_max, joint_sum, joint_out = merge_pair(
        (cache_max, cache_sum, cache_out), (new_max, new_sum, new_out)
    )
    attended = (
        (joint_out / joint_sum[..., None])
        .astype(jnp.bfloat16)
        .reshape(requests, steps_count, local_width)
    )
    head_terms = jnp.einsum("rtc,cd->rtd", attended, w_out, preferred_element_type=jnp.float32)
    summed = lax.psum(head_terms, "head")
    inputs_all = gathered[:, :, 3 * local_width :]
    normed_all = layer_norm(
        inputs_all.astype(jnp.float32) + summed + out_bias, attn_gain, attn_shift
    ).astype(jnp.bfloat16)
    hidden_all = jax.nn.gelu(
        jnp.einsum("rtd,df->rtf", normed_all, w_up, preferred_element_type=jnp.float32) + up_bias,
        approximate=False,
    ).astype(jnp.bfloat16)
    normed = lax.dynamic_slice_in_dim(normed_all, lax.axis_index("head") * own_rows, own_rows, 0)
    reduced = lax.psum_scatter(
        jnp.einsum("rtf,fd->rtd", hidden_all, w_down, preferred_element_type=jnp.float32),
        "head",
        scatter_dimension=0,
        tiled=True,
    )
    return layer_norm(normed.astype(jnp.float32) + reduced + down_bias, ffn_gain, ffn_shift).astype(
        jnp.bfloat16
    )


def solution(mesh):
    placed = (
        P("head", None, None),
        P(None, "seq", "head"),
        P(None, "seq", "head"),
        P(None, "seq", None),
        P(None, "seq"),
        P(),
        P(),
        P(None, None, "head"),
        P(None, "head"),
        P("head", None),
        P(),
        P(),
        P(),
        P(None, "head"),
        P("head"),
        P("head", None),
        P(),
        P(),
        P(),
    )
    return jax.shard_map(
        on_device, mesh=mesh, in_specs=placed, out_specs=P("head", None, None), check_vma=False
    )
```

profile of v0, /device:TPU:8, one launch (start us, length us, event | category | flops | bytes accessed | tf_op | source)
XLA Modules:
  0.0 232.6 jit_solution(7463980318247415298)
XLA Ops:
  6.5 0.8 broadcast_compare_fusion
  7.3 0.7 slice_bitcast_fusion
  8.0 0.7 broadcast_subtract_fusion
  9.0 1.0 copy.122
  10.0 13.1 %all_gather.3 = bf16[64,4,1024]{2,0,1:T(8,128)(2,1)S(1)} all-gather(bf16[16,4,1024]{2,0,1:T(8,128)(2,1)S(1)} %copy.122), channel_id=1, replica_groups=mesh['seq'=128,'head'=4] {'head'}, dimensions={0}, use_global_device_ids=true | all-gather | bytes 655360 | tf_op jit(solution)/shard_map/all_gather | solution.py:101
  23.1 0.4 fusion.7
  23.6 0.7 fusion.131
  24.3 0.8 reshape.249
  25.0 0.3 fusion.8
  25.3 0.7 copy-done.18
  26.1 0.9 fusion
  27.0 0.4 reshape.247
  27.7 1.7 select_reduce_fusion
  29.4 0.5 copy.131
  29.9 0.4 convert_reduce_fusion
  30.4 0.5 copy.132
  31.2 0.4 reshape.250
  31.6 0.4 convolution_bitcast_fusion.1
  32.4 1.9 collective-permute-start
  34.3 1.3 collective-permute-done
  36.4 3.8 %collective-permute-start.1 = (f32[264,128]{1,0:T(8,128)S(1)}, f32[264,128]{1,0:T(8,128)S(1)}, u32[]{:S(2)}, u32[]{:S(2)}) collective-permute-start(f32[264,128]{1,0:T(8,128)S(1)} %pad_maximum_fusion.1), channel_id=1, source_target_pairs={{0,8},{4,12},{8,0},{12,4},{16,24},{20,28},{24,16},{28,20},{32,40},... | collective-permute-start | bytes 405512 | tf_op jit(solution)/shard_map/ppermute | solution.py:58
  40.3 3.9 %collective-permute-done.1 = f32[264,128]{1,0:T(8,128)S(1)} collective-permute-done((f32[264,128]{1,0:T(8,128)S(1)}, f32[264,128]{1,0:T(8,128)S(1)}, u32[]{:S(2)}, u32[]{:S(2)}) %collective-permute-start.1) | collective-permute-done | bytes 135200 | tf_op jit(solution)/shard_map/ppermute | solution.py:58
  44.9 5.2 %collective-permute-start.2 = (f32[264,128]{1,0:T(8,128)S(1)}, f32[264,128]{1,0:T(8,128)S(1)}, u32[]{:S(2)}, u32[]{:S(2)}) collective-permute-start(f32[264,128]{1,0:T(8,128)S(1)} %pad_maximum_fusion.2), channel_id=1, source_target_pairs={{0,16},{4,20},{8,24},{12,28},{16,0},{20,4},{24,8},{28,12},{32,48},... | collective-permute-start | bytes 405512 | tf_op jit(solution)/shard_map/ppermute | solution.py:58
  50.1 6.1 %collective-permute-done.2 = f32[264,128]{1,0:T(8,128)S(1)} collective-permute-done((f32[264,128]{1,0:T(8,128)S(1)}, f32[264,128]{1,0:T(8,128)S(1)}, u32[]{:S(2)}, u32[]{:S(2)}) %collective-permute-start.2) | collective-permute-done | bytes 135200 | tf_op jit(solution)/shard_map/ppermute | solution.py:58
  57.0 9.1 %collective-permute-start.3 = (f32[264,128]{1,0:T(8,128)S(1)}, f32[264,128]{1,0:T(8,128)S(1)}, u32[]{:S(2)}, u32[]{:S(2)}) collective-permute-start(f32[264,128]{1,0:T(8,128)S(1)} %pad_maximum_fusion.3), channel_id=1, source_target_pairs={{0,32},{4,36},{8,40},{12,44},{16,48},{20,52},{24,56},{28,60},{32,0... | collective-permute-start | bytes 405512 | tf_op jit(solution)/shard_map/ppermute | solution.py:58
  66.2 10.2 %collective-permute-done.3 = f32[264,128]{1,0:T(8,128)S(1)} collective-permute-done((f32[264,128]{1,0:T(8,128)S(1)}, f32[264,128]{1,0:T(8,128)S(1)}, u32[]{:S(2)}, u32[]{:S(2)}) %collective-permute-start.3) | collective-permute-done | bytes 135200 | tf_op jit(solution)/shard_map/ppermute | solution.py:58
  77.1 13.6 %collective-permute-start.4 = (f32[264,128]{1,0:T(8,128)S(1)}, f32[264,128]{1,0:T(8,128)S(1)}, u32[]{:S(2)}, u32[]{:S(2)}) collective-permute-start(f32[264,128]{1,0:T(8,128)S(1)} %pad_maximum_fusion.4), channel_id=1, source_target_pairs={{0,64},{4,68},{8,72},{12,76},{16,80},{20,84},{24,88},{28,92},{32,9... | collective-permute-start | bytes 405512 | tf_op jit(solution)/shard_map/ppermute | solution.py:58
  91.0 12.1 %collective-permute-done.4 = f32[264,128]{1,0:T(8,128)S(1)} collective-permute-done((f32[264,128]{1,0:T(8,128)S(1)}, f32[264,128]{1,0:T(8,128)S(1)}, u32[]{:S(2)}, u32[]{:S(2)}) %collective-permute-start.4) | collective-permute-done | bytes 135200 | tf_op jit(solution)/shard_map/ppermute | solution.py:58
  103.9 3.5 %collective-permute-start.5 = (f32[264,128]{1,0:T(8,128)S(1)}, f32[264,128]{1,0:T(8,128)S(1)}, u32[]{:S(2)}, u32[]{:S(2)}) collective-permute-start(f32[264,128]{1,0:T(8,128)S(1)} %pad_maximum_fusion.5), channel_id=1, source_target_pairs={{0,128},{4,132},{8,136},{12,140},{16,144},{20,148},{24,152},{28,15... | collective-permute-start | bytes 405512 | tf_op jit(solution)/shard_map/ppermute | solution.py:58
  107.8 3.3 %collective-permute-done.5 = f32[264,128]{1,0:T(8,128)S(1)} collective-permute-done((f32[264,128]{1,0:T(8,128)S(1)}, f32[264,128]{1,0:T(8,128)S(1)}, u32[]{:S(2)}, u32[]{:S(2)}) %collective-permute-start.5) | collective-permute-done | bytes 135200 | tf_op jit(solution)/shard_map/ppermute | solution.py:58
  111.9 3.9 %collective-permute-start.6 = (f32[264,128]{1,0:T(8,128)S(1)}, f32[264,128]{1,0:T(8,128)S(1)}, u32[]{:S(2)}, u32[]{:S(2)}) collective-permute-start(f32[264,128]{1,0:T(8,128)S(1)} %pad_maximum_fusion.6), channel_id=1, source_target_pairs={{0,256},{4,260},{8,264},{12,268},{16,272},{20,276},{24,280},{28,28... | collective-permute-start | bytes 405512 | tf_op jit(solution)/shard_map/ppermute | solution.py:58
  116.1 4.2 %collective-permute-done.6 = f32[264,128]{1,0:T(8,128)S(1)} collective-permute-done((f32[264,128]{1,0:T(8,128)S(1)}, f32[264,128]{1,0:T(8,128)S(1)}, u32[]{:S(2)}, u32[]{:S(2)}) %collective-permute-start.6) | collective-permute-done | bytes 135200 | tf_op jit(solution)/shard_map/ppermute | solution.py:58
  122.3 0.5 fusion.6
  123.0 0.7 copy-done.6
  123.7 1.3 fusion.29
  125.3 58.1 %all-reduce.2.cloned.1.call-done = f32[64,4,1024]{2,0,1:T(8,128)} async-done(((f32[64,4,1024]{2,0,1:T(8,128)}), f32[64,4,1024]{2,0,1:T(8,128)}) %all-reduce.2.cloned.1.call-update) | async-done | bytes 1048592 | tf_op jit(solution)/shard_map/psum | solution.py:146
  183.4 1.5 fusion.26
  185.0 0.3 multiply_reduce_fusion
  185.3 0.4 copy-done.11
  185.7 0.3 copy-done.10
  186.0 0.3 add_convert_fusion
  186.3 0.9 copy-done.16
  187.2 0.6 fusion.75
  187.8 2.5 %fusion.9 = f32[64,4,1024]{2,0,1:T(8,128)} fusion(bf16[512,1024]{1,0:T(8,128)(2,1)S(1)} %copy-done, f32[64,4,512]{2,0,1:T(8,128)S(1)} %get-tuple-element.45, u8[64,512]{1,0:T(8,128)(4,1)S(1)} %get-tuple-element.6, u8[64,512]{1,0:T(8,128)(4,1)S(1)} %get-tuple-element.5), kind=kOutput, calls=%fused_computation.16 | convolution fusion | flops 277610496 | bytes 2686976 | tf_op jit(solution)/shard_map/rtf,fd->rtd/dot_general | solution.py:157
  190.3 32.6 %reduce-scatter.2.cloned.1.call-done = f32[16,4,1024]{2,0,1:T(8,128)} async-done(((f32[64,4,1024]{2,0,1:T(8,128)}), f32[16,4,1024]{2,0,1:T(8,128)}) %reduce-scatter.2.cloned.1.call-update) | async-done | bytes 262160 | tf_op jit(solution)/shard_map/reduce_scatter | solution.py:156
  222.9 1.1 fusion.82
  224.2 0.7 copy-done.12
  225.0 0.8 copy.180
  (149 shorter events, 9.3 us)
Async XLA Ops:
  6.5 181.2 %copy-start = (bf16[512,1024]{1,0:T(8,128)(2,1)S(1)}, bf16[512,1024]{1,0:T(8,128)(2,1)}, u32[]{:S(2)}) copy-start(bf16[512,1024]{1,0:T(8,128)(2,1)} %param.34) | copy-start | bytes 3145732
  6.5 16.6 %copy-start.3 = (bf16[3,1024,128]{2,1,0:T(8,128)(2,1)S(1)}, bf16[3,1024,128]{2,1,0:T(8,128)(2,1)}, u32[]{:S(2)}) copy-start(bf16[3,1024,128]{2,1,0:T(8,128)(2,1)} %param.26) | copy-start | bytes 2359300
  6.5 176.9 %all-reduce.2.cloned.1.call-start = ((), (), s32[]{:S(2)}) async-start(), calls=%async_computation.1 | async-start | bytes 2097152 | tf_op jit(solution)/shard_map/psum | solution.py:146
  9.9 13.2 %copy-start.14 = (f32[3,128]{1,0:T(4,128)S(1)}, f32[3,128]{1,0:T(4,128)}, u32[]{:S(2)}) copy-start(f32[3,128]{1,0:T(4,128)} %param.27) | copy-start | bytes 4612
  23.5 1.5 copy-start.17
  25.0 1.0 copy-start.18
  27.0 0.7 copy-start.15
  29.4 1.8 copy-start.4
  32.4 3.2 %collective-permute-start = (f32[264,128]{1,0:T(8,128)S(1)}, f32[264,128]{1,0:T(8,128)S(1)}, u32[]{:S(2)}, u32[]{:S(2)}) collective-permute-start(f32[264,128]{1,0:T(8,128)S(1)} %pad_maximum_fusion), channel_id=1, source_target_pairs={{0,4},{4,0},{8,12},{12,8},{16,20},{20,16},{24,28},{28,24},{32,36},... | collective-permute-start | bytes 405512 | tf_op jit(solution)/shard_map/ppermute | solution.py:58
  36.4 7.7 %collective-permute-start.1 = (f32[264,128]{1,0:T(8,128)S(1)}, f32[264,128]{1,0:T(8,128)S(1)}, u32[]{:S(2)}, u32[]{:S(2)}) collective-permute-start(f32[264,128]{1,0:T(8,128)S(1)} %pad_maximum_fusion.1), channel_id=1, source_target_pairs={{0,8},{4,12},{8,0},{12,4},{16,24},{20,28},{24,16},{28,20},{32,40},... | collective-permute-start | bytes 405512 | tf_op jit(solution)/shard_map/ppermute | solution.py:58
  44.9 11.3 %collective-permute-start.2 = (f32[264,128]{1,0:T(8,128)S(1)}, f32[264,128]{1,0:T(8,128)S(1)}, u32[]{:S(2)}, u32[]{:S(2)}) collective-permute-start(f32[264,128]{1,0:T(8,128)S(1)} %pad_maximum_fusion.2), channel_id=1, source_target_pairs={{0,16},{4,20},{8,24},{12,28},{16,0},{20,4},{24,8},{28,12},{32,48},... | collective-permute-start | bytes 405512 | tf_op jit(solution)/shard_map/ppermute | solution.py:58
  56.9 9.1 %copy-start.5 = (bf16[64,4,128]{2,0,1:T(8,128)(2,1)S(1)}, bf16[64,4,128]{2,0,1:T(8,128)(2,1)}, u32[]{:S(2)}) copy-start(bf16[64,4,128]{2,0,1:T(8,128)(2,1)} %get-tuple-element.41) | copy-start | bytes 196612
  57.0 19.4 %collective-permute-start.3 = (f32[264,128]{1,0:T(8,128)S(1)}, f32[264,128]{1,0:T(8,128)S(1)}, u32[]{:S(2)}, u32[]{:S(2)}) collective-permute-start(f32[264,128]{1,0:T(8,128)S(1)} %pad_maximum_fusion.3), channel_id=1, source_target_pairs={{0,32},{4,36},{8,40},{12,44},{16,48},{20,52},{24,56},{28,60},{32,0... | collective-permute-start | bytes 405512 | tf_op jit(solution)/shard_map/ppermute | solution.py:58
  77.1 13.6 %copy-start.7 = (bf16[64,4,2,64]{3,2,0,1:T(2,128)(2,1)S(1)}, bf16[64,4,2,64]{3,2,0,1:T(2,128)(2,1)}, u32[]{:S(2)}) copy-start(bf16[64,4,2,64]{3,2,0,1:T(2,128)(2,1)} %reshape.249) | copy-start | bytes 196612
  77.1 26.0 %collective-permute-start.4 = (f32[264,128]{1,0:T(8,128)S(1)}, f32[264,128]{1,0:T(8,128)S(1)}, u32[]{:S(2)}, u32[]{:S(2)}) collective-permute-start(f32[264,128]{1,0:T(8,128)S(1)} %pad_maximum_fusion.4), channel_id=1, source_target_pairs={{0,64},{4,68},{8,72},{12,76},{16,80},{20,84},{24,88},{28,92},{32,9... | collective-permute-start | bytes 405512 | tf_op jit(solution)/shard_map/ppermute | solution.py:58
  103.9 7.2 %collective-permute-start.5 = (f32[264,128]{1,0:T(8,128)S(1)}, f32[264,128]{1,0:T(8,128)S(1)}, u32[]{:S(2)}, u32[]{:S(2)}) collective-permute-start(f32[264,128]{1,0:T(8,128)S(1)} %pad_maximum_fusion.5), channel_id=1, source_target_pairs={{0,128},{4,132},{8,136},{12,140},{16,144},{20,148},{24,152},{28,15... | collective-permute-start | bytes 405512 | tf_op jit(solution)/shard_map/ppermute | solution.py:58
  111.9 8.4 %collective-permute-start.6 = (f32[264,128]{1,0:T(8,128)S(1)}, f32[264,128]{1,0:T(8,128)S(1)}, u32[]{:S(2)}, u32[]{:S(2)}) collective-permute-start(f32[264,128]{1,0:T(8,128)S(1)} %pad_maximum_fusion.6), channel_id=1, source_target_pairs={{0,256},{4,260},{8,264},{12,268},{16,272},{20,276},{24,280},{28,28... | collective-permute-start | bytes 405512 | tf_op jit(solution)/shard_map/ppermute | solution.py:58
  122.8 1.0 copy-start.6
  125.1 58.4 %copy-start.8 = (f32[1024]{0:T(1024)S(1)}, f32[1024]{0:T(1024)}, u32[]{:S(2)}) copy-start(f32[1024]{0:T(1024)} %param.29) | copy-start | bytes 12292
  125.1 97.8 %reduce-scatter.2.cloned.1.call-start = ((), (), s32[]{:S(2)}) async-start(), calls=%async_computation.2 | async-start | bytes 1310720 | tf_op jit(solution)/shard_map/reduce_scatter | solution.py:156
  183.4 1.5 copy-start.1
  185.0 0.7 copy-start.11
  185.3 0.7 copy-start.10
  186.0 1.2 copy-start.16
  186.0 1.2 copy-start.19
  190.3 32.6 %copy-start.9 = (f32[1024]{0:T(1024)S(1)}, f32[1024]{0:T(1024)}, u32[]{:S(2)}) copy-start(f32[1024]{0:T(1024)} %param.35) | copy-start | bytes 12292
  222.9 1.1 copy-start.2
  222.9 1.4 copy-start.13
  224.2 0.7 copy-start.12
Sparse Core Ops, SparseCore 0:
  125.2 58.1 all-reduce.1
  190.4 32.4 reduce-scatter.1
where the time goes:
time: 233 us
  waiting for transfers between devices  132 us (57%)
  starting transfers between devices  41.2 us (18%)
  local copies, waits for them, and re-layouts  16.8 us (7%)
  between operations  14.3 us (6%)
  blocking collectives  13.1 us (6%)
  matrix products  8.92 us (4%)
  other arithmetic  6.39 us (3%)
    psum x1, waiting for transfers between devices, on_device(): summed = lax.psum(head_terms, 'head')  58.1 us
    ppermute x7, waiting for transfers between devices, seq_merge(): other = lax.ppermute(packed, 'seq', pairs)  41.2 us
    ppermute x7, starting transfers between devices, seq_merge(): other = lax.ppermute(packed, 'seq', pairs)  41 us
    reduce_scatter x1, waiting for transfers between devices, on_device(): lax.psum_scatter(jnp.einsum('rtf,fd->rtd', hidden_all, w_down, preferred_...  32.6 us
    all_gather x1, blocking collectives, on_device(): block_rows = lax.all_gather(tokens, 'head', axis=0, tiled=True)  13.1 us
    unnamed x41, local copies, waits for them, and re-layouts  4.99 us
  transfers between devices with their start and end apart: 9, of which 9 were waited for; matrix products, arithmetic and copies ran while one was open for 0% of the time, Pallas kernels for 0%

commit v1 on v0

--- a/solution.py
+++ b/solution.py
@@ -143,7 +143,20 @@
         .reshape(requests, steps_count, local_width)
     )
     head_terms = jnp.einsum("rtc,cd->rtd", attended, w_out, preferred_element_type=jnp.float32)
-    summed = lax.psum(head_terms, "head")
+
+    def list_inputs(link_axis, raw):
+        dev_count = lax.axis_size(link_axis)
+
+        def _enter_masks(carry_in, work_now):
+            if work_now >= dev_count:
+                return carry_in
+            oldest = tuple(((rr, rr ^ work_now) for rr in range(dev_count)))
+            w1 = lax.ppermute(carry_in, link_axis, oldest)
+            return _enter_masks(carry_in + w1, 2 * work_now)
+
+        return _enter_masks(raw, 1)
+
+    summed = list_inputs("head", head_terms)
     inputs_all = gathered[:, :, 3 * local_width :]
     normed_all = layer_norm(
         inputs_all.astype(jnp.float32) + summed + out_bias, attn_gain, attn_shift

time: 233 us -> 219 us (0.940)
  waiting for transfers between devices: 132 us -> 113 us
  starting transfers between devices: 41.2 us -> 48.2 us
    psum x1 -> x0, waiting for transfers between devices: 58.1 us -> none  [on_device(): summed = lax.psum(head_terms, 'head')]
    ppermute x0 -> x2, waiting for transfers between devices: none -> 43.1 us  [_enter_masks(): w1 = lax.ppermute(carry_in, link_axis, oldest)]
    ppermute x0 -> x2, starting transfers between devices: none -> 7.16 us  [_enter_masks(): w1 = lax.ppermute(carry_in, link_axis, oldest)]
    reduce_scatter x1, waiting for transfers between devices: 32.6 us -> 28.5 us  [on_device(): lax.psum_scatter(jnp.einsum('rtf,fd->rtd', hidden_all, w_down, preferred_...]
    unnamed x41 -> x39, local copies, waits for them, and re-layouts: 4.99 us -> 4.53 us
  transfers between devices with their start and end apart: 9 -> 10, of which waited for: 9 -> 10; matrix products, arithmetic and copies ran while one was open for 0% -> 0% of each run, Pallas kernels for 0% -> 0%
where the time goes in v1:
time: 219 us; the launch traced here: 218 us
  waiting for transfers between devices  113 us (52%)
  starting transfers between devices  48.2 us (22%)
  local copies, waits for them, and re-layouts  16.4 us (7%)
  between operations  14.3 us (7%)
  blocking collectives  13.1 us (6%)
  matrix products  7.9 us (4%)
  other arithmetic  5.2 us (2%)
    ppermute x2, waiting for transfers between devices, _enter_masks(): w1 = lax.ppermute(carry_in, link_axis, oldest)  43.1 us
    ppermute x7, waiting for transfers between devices, seq_merge(): other = lax.ppermute(packed, 'seq', pairs)  41.2 us
    ppermute x7, starting transfers between devices, seq_merge(): other = lax.ppermute(packed, 'seq', pairs)  41 us
    reduce_scatter x1, waiting for transfers between devices, on_device(): lax.psum_scatter(jnp.einsum('rtf,fd->rtd', hidden_all, w_down, preferred_...  28.5 us
    all_gather x1, blocking collectives, on_device(): block_rows = lax.all_gather(tokens, 'head', axis=0, tiled=True)  13.1 us
    ppermute x2, starting transfers between devices, _enter_masks(): w1 = lax.ppermute(carry_in, link_axis, oldest)  7.16 us
    unnamed x39, local copies, waits for them, and re-layouts  4.53 us
  transfers between devices with their start and end apart: 10, of which 10 were waited for; matrix products, arithmetic and copies ran while one was open for 0% of the time, Pallas kernels for 0%

profile of v1, /device:TPU:8, one launch (start us, length us, event | category | flops | bytes accessed | tf_op | source)
XLA Modules:
  0.0 217.9 jit_solution(17954690829291659920)
XLA Ops:
  6.5 0.8 broadcast_compare_fusion
  7.3 0.7 slice_bitcast_fusion
  8.0 0.7 broadcast_subtract_fusion
  9.0 1.0 copy.122
  10.0 13.1 %all_gather.3 = bf16[64,4,1024]{2,0,1:T(8,128)(2,1)S(1)} all-gather(bf16[16,4,1024]{2,0,1:T(8,128)(2,1)S(1)} %copy.122), channel_id=1, replica_groups=mesh['seq'=128,'head'=4] {'head'}, dimensions={0}, use_global_device_ids=true | all-gather | bytes 655360 | tf_op jit(solution)/shard_map/all_gather | solution.py:101
  23.1 0.4 fusion.7
  23.6 0.7 fusion.131
  24.3 0.8 reshape.249
  25.0 0.3 fusion.8
  25.3 0.7 copy-done.17
  26.1 0.9 fusion
  27.0 0.4 reshape.247
  27.7 1.7 select_reduce_fusion
  29.4 0.5 copy.131
  29.9 0.4 convert_reduce_fusion
  30.4 0.5 copy.132
  31.2 0.4 reshape.250
  31.6 0.4 convolution_bitcast_fusion.1
  32.4 1.9 collective-permute-start
  34.3 1.3 collective-permute-done
  36.4 3.8 %collective-permute-start.1 = (f32[264,128]{1,0:T(8,128)S(1)}, f32[264,128]{1,0:T(8,128)S(1)}, u32[]{:S(2)}, u32[]{:S(2)}) collective-permute-start(f32[264,128]{1,0:T(8,128)S(1)} %pad_maximum_fusion.1), channel_id=1, source_target_pairs={{0,8},{4,12},{8,0},{12,4},{16,24},{20,28},{24,16},{28,20},{32,40},... | collective-permute-start | bytes 405512 | tf_op jit(solution)/shard_map/ppermute | solution.py:58
  40.3 3.9 %collective-permute-done.1 = f32[264,128]{1,0:T(8,128)S(1)} collective-permute-done((f32[264,128]{1,0:T(8,128)S(1)}, f32[264,128]{1,0:T(8,128)S(1)}, u32[]{:S(2)}, u32[]{:S(2)}) %collective-permute-start.1) | collective-permute-done | bytes 135200 | tf_op jit(solution)/shard_map/ppermute | solution.py:58
  44.9 5.2 %collective-permute-start.2 = (f32[264,128]{1,0:T(8,128)S(1)}, f32[264,128]{1,0:T(8,128)S(1)}, u32[]{:S(2)}, u32[]{:S(2)}) collective-permute-start(f32[264,128]{1,0:T(8,128)S(1)} %pad_maximum_fusion.2), channel_id=1, source_target_pairs={{0,16},{4,20},{8,24},{12,28},{16,0},{20,4},{24,8},{28,12},{32,48},... | collective-permute-start | bytes 405512 | tf_op jit(solution)/shard_map/ppermute | solution.py:58
  50.1 6.1 %collective-permute-done.2 = f32[264,128]{1,0:T(8,128)S(1)} collective-permute-done((f32[264,128]{1,0:T(8,128)S(1)}, f32[264,128]{1,0:T(8,128)S(1)}, u32[]{:S(2)}, u32[]{:S(2)}) %collective-permute-start.2) | collective-permute-done | bytes 135200 | tf_op jit(solution)/shard_map/ppermute | solution.py:58
  57.0 9.1 %collective-permute-start.3 = (f32[264,128]{1,0:T(8,128)S(1)}, f32[264,128]{1,0:T(8,128)S(1)}, u32[]{:S(2)}, u32[]{:S(2)}) collective-permute-start(f32[264,128]{1,0:T(8,128)S(1)} %pad_maximum_fusion.3), channel_id=1, source_target_pairs={{0,32},{4,36},{8,40},{12,44},{16,48},{20,52},{24,56},{28,60},{32,0... | collective-permute-start | bytes 405512 | tf_op jit(solution)/shard_map/ppermute | solution.py:58
  66.2 10.2 %collective-permute-done.3 = f32[264,128]{1,0:T(8,128)S(1)} collective-permute-done((f32[264,128]{1,0:T(8,128)S(1)}, f32[264,128]{1,0:T(8,128)S(1)}, u32[]{:S(2)}, u32[]{:S(2)}) %collective-permute-start.3) | collective-permute-done | bytes 135200 | tf_op jit(solution)/shard_map/ppermute | solution.py:58
  77.1 13.6 %collective-permute-start.4 = (f32[264,128]{1,0:T(8,128)S(1)}, f32[264,128]{1,0:T(8,128)S(1)}, u32[]{:S(2)}, u32[]{:S(2)}) collective-permute-start(f32[264,128]{1,0:T(8,128)S(1)} %pad_maximum_fusion.4), channel_id=1, source_target_pairs={{0,64},{4,68},{8,72},{12,76},{16,80},{20,84},{24,88},{28,92},{32,9... | collective-permute-start | bytes 405512 | tf_op jit(solution)/shard_map/ppermute | solution.py:58
  91.0 12.1 %collective-permute-done.4 = f32[264,128]{1,0:T(8,128)S(1)} collective-permute-done((f32[264,128]{1,0:T(8,128)S(1)}, f32[264,128]{1,0:T(8,128)S(1)}, u32[]{:S(2)}, u32[]{:S(2)}) %collective-permute-start.4) | collective-permute-done | bytes 135200 | tf_op jit(solution)/shard_map/ppermute | solution.py:58
  103.9 3.5 %collective-permute-start.5 = (f32[264,128]{1,0:T(8,128)S(1)}, f32[264,128]{1,0:T(8,128)S(1)}, u32[]{:S(2)}, u32[]{:S(2)}) collective-permute-start(f32[264,128]{1,0:T(8,128)S(1)} %pad_maximum_fusion.5), channel_id=1, source_target_pairs={{0,128},{4,132},{8,136},{12,140},{16,144},{20,148},{24,152},{28,15... | collective-permute-start | bytes 405512 | tf_op jit(solution)/shard_map/ppermute | solution.py:58
  107.8 3.3 %collective-permute-done.5 = f32[264,128]{1,0:T(8,128)S(1)} collective-permute-done((f32[264,128]{1,0:T(8,128)S(1)}, f32[264,128]{1,0:T(8,128)S(1)}, u32[]{:S(2)}, u32[]{:S(2)}) %collective-permute-start.5) | collective-permute-done | bytes 135200 | tf_op jit(solution)/shard_map/ppermute | solution.py:58
  111.9 3.9 %collective-permute-start.6 = (f32[264,128]{1,0:T(8,128)S(1)}, f32[264,128]{1,0:T(8,128)S(1)}, u32[]{:S(2)}, u32[]{:S(2)}) collective-permute-start(f32[264,128]{1,0:T(8,128)S(1)} %pad_maximum_fusion.6), channel_id=1, source_target_pairs={{0,256},{4,260},{8,264},{12,268},{16,272},{20,276},{24,280},{28,28... | collective-permute-start | bytes 405512 | tf_op jit(solution)/shard_map/ppermute | solution.py:58
  116.1 4.2 %collective-permute-done.6 = f32[264,128]{1,0:T(8,128)S(1)} collective-permute-done((f32[264,128]{1,0:T(8,128)S(1)}, f32[264,128]{1,0:T(8,128)S(1)}, u32[]{:S(2)}, u32[]{:S(2)}) %collective-permute-start.6) | collective-permute-done | bytes 135200 | tf_op jit(solution)/shard_map/ppermute | solution.py:58
  122.3 0.5 fusion.6
  123.0 0.7 copy-done.5
  123.7 0.3 fusion.28
  124.0 3.4 %collective-permute-start.7 = (f32[64,4,1024]{2,0,1:T(8,128)S(1)}, f32[64,4,1024]{2,0,1:T(8,128)S(1)}, u32[]{:S(2)}, u32[]{:S(2)}) collective-permute-start(f32[64,4,1024]{2,0,1:T(8,128)S(1)} %fusion.28), channel_id=1, source_target_pairs={{0,1},{1,0},{2,3},{3,2},{4,5},{5,4},{6,7},{7,6},{8,9},{9,8},{10,11... | collective-permute-start | bytes 3145736 | tf_op jit(solution)/shard_map/ppermute | solution.py:154
  127.4 21.4 %collective-permute-done.7 = f32[64,4,1024]{2,0,1:T(8,128)S(1)} collective-permute-done((f32[64,4,1024]{2,0,1:T(8,128)S(1)}, f32[64,4,1024]{2,0,1:T(8,128)S(1)}, u32[]{:S(2)}, u32[]{:S(2)}) %collective-permute-start.7) | collective-permute-done | bytes 1048608 | tf_op jit(solution)/shard_map/ppermute | solution.py:154
  149.0 3.8 %collective-permute-start.8 = (f32[64,4,1024]{2,0,1:T(8,128)S(1)}, f32[64,4,1024]{2,0,1:T(8,128)S(1)}, u32[]{:S(2)}, u32[]{:S(2)}) collective-permute-start(f32[64,4,1024]{2,0,1:T(8,128)S(1)} %add.182), channel_id=1, source_target_pairs={{0,2},{1,3},{2,0},{3,1},{4,6},{5,7},{6,4},{7,5},{8,10},{9,11},{10,... | collective-permute-start | bytes 3145736 | tf_op jit(solution)/shard_map/ppermute | solution.py:154
  152.8 21.7 %collective-permute-done.8 = f32[64,4,1024]{2,0,1:T(8,128)S(1)} collective-permute-done((f32[64,4,1024]{2,0,1:T(8,128)S(1)}, f32[64,4,1024]{2,0,1:T(8,128)S(1)}, u32[]{:S(2)}, u32[]{:S(2)}) %collective-permute-start.8) | collective-permute-done | bytes 1048608 | tf_op jit(solution)/shard_map/ppermute | solution.py:154
  174.4 0.3 fusion.127
  175.0 0.4 copy-done.9
  175.9 0.3 copy-done.15
  176.4 0.6 fusion.74
  177.0 2.5 %fusion.9 = f32[64,4,1024]{2,0,1:T(8,128)} fusion(bf16[512,1024]{1,0:T(8,128)(2,1)S(1)} %copy-done, f32[64,4,512]{2,0,1:T(8,128)S(1)} %get-tuple-element.47, u8[64,512]{1,0:T(8,128)(4,1)S(1)} %get-tuple-element.6, u8[64,512]{1,0:T(8,128)(4,1)S(1)} %get-tuple-element.5), kind=kOutput, calls=%fused_computation.16 | convolution fusion | flops 277610496 | bytes 2686976 | tf_op jit(solution)/shard_map/rtf,fd->rtd/dot_general | solution.py:170
  179.6 28.5 %reduce-scatter.2.cloned.1.call-done = f32[16,4,1024]{2,0,1:T(8,128)} async-done(((f32[64,4,1024]{2,0,1:T(8,128)}), f32[16,4,1024]{2,0,1:T(8,128)}) %reduce-scatter.2.cloned.1.call-update) | async-done | bytes 262160 | tf_op jit(solution)/shard_map/reduce_scatter | solution.py:169
  208.1 1.1 fusion.81
  209.5 0.7 copy-done.10
  210.2 0.8 copy.180
  (149 shorter events, 10.1 us)
Async XLA Ops:
  6.5 170.5 %copy-start = (bf16[512,1024]{1,0:T(8,128)(2,1)S(1)}, bf16[512,1024]{1,0:T(8,128)(2,1)}, u32[]{:S(2)}) copy-start(bf16[512,1024]{1,0:T(8,128)(2,1)} %param.34) | copy-start | bytes 3145732
  6.5 16.6 %copy-start.2 = (bf16[3,1024,128]{2,1,0:T(8,128)(2,1)S(1)}, bf16[3,1024,128]{2,1,0:T(8,128)(2,1)}, u32[]{:S(2)}) copy-start(bf16[3,1024,128]{2,1,0:T(8,128)(2,1)} %param.26) | copy-start | bytes 2359300
  6.5 201.6 %reduce-scatter.2.cloned.1.call-start = ((), (), s32[]{:S(2)}) async-start(), calls=%async_computation.1 | async-start | bytes 1310720 | tf_op jit(solution)/shard_map/reduce_scatter | solution.py:169
  9.9 13.2 %copy-start.13 = (f32[3,128]{1,0:T(4,128)S(1)}, f32[3,128]{1,0:T(4,128)}, u32[]{:S(2)}) copy-start(f32[3,128]{1,0:T(4,128)} %param.27) | copy-start | bytes 4612
  23.5 1.5 copy-start.16
  25.0 1.0 copy-start.17
  27.0 0.7 copy-start.14
  29.4 1.8 copy-start.3
  32.4 3.2 %collective-permute-start = (f32[264,128]{1,0:T(8,128)S(1)}, f32[264,128]{1,0:T(8,128)S(1)}, u32[]{:S(2)}, u32[]{:S(2)}) collective-permute-start(f32[264,128]{1,0:T(8,128)S(1)} %pad_maximum_fusion), channel_id=1, source_target_pairs={{0,4},{4,0},{8,12},{12,8},{16,20},{20,16},{24,28},{28,24},{32,36},... | collective-permute-start | bytes 405512 | tf_op jit(solution)/shard_map/ppermute | solution.py:58
  36.4 7.7 %collective-permute-start.1 = (f32[264,128]{1,0:T(8,128)S(1)}, f32[264,128]{1,0:T(8,128)S(1)}, u32[]{:S(2)}, u32[]{:S(2)}) collective-permute-start(f32[264,128]{1,0:T(8,128)S(1)} %pad_maximum_fusion.1), channel_id=1, source_target_pairs={{0,8},{4,12},{8,0},{12,4},{16,24},{20,28},{24,16},{28,20},{32,40},... | collective-permute-start | bytes 405512 | tf_op jit(solution)/shard_map/ppermute | solution.py:58
  44.9 11.3 %collective-permute-start.2 = (f32[264,128]{1,0:T(8,128)S(1)}, f32[264,128]{1,0:T(8,128)S(1)}, u32[]{:S(2)}, u32[]{:S(2)}) collective-permute-start(f32[264,128]{1,0:T(8,128)S(1)} %pad_maximum_fusion.2), channel_id=1, source_target_pairs={{0,16},{4,20},{8,24},{12,28},{16,0},{20,4},{24,8},{28,12},{32,48},... | collective-permute-start | bytes 405512 | tf_op jit(solution)/shard_map/ppermute | solution.py:58
  56.9 9.1 %copy-start.4 = (bf16[64,4,128]{2,0,1:T(8,128)(2,1)S(1)}, bf16[64,4,128]{2,0,1:T(8,128)(2,1)}, u32[]{:S(2)}) copy-start(bf16[64,4,128]{2,0,1:T(8,128)(2,1)} %get-tuple-element.43) | copy-start | bytes 196612
  57.0 19.4 %collective-permute-start.3 = (f32[264,128]{1,0:T(8,128)S(1)}, f32[264,128]{1,0:T(8,128)S(1)}, u32[]{:S(2)}, u32[]{:S(2)}) collective-permute-start(f32[264,128]{1,0:T(8,128)S(1)} %pad_maximum_fusion.3), channel_id=1, source_target_pairs={{0,32},{4,36},{8,40},{12,44},{16,48},{20,52},{24,56},{28,60},{32,0... | collective-permute-start | bytes 405512 | tf_op jit(solution)/shard_map/ppermute | solution.py:58
  77.1 13.6 %copy-start.6 = (bf16[64,4,2,64]{3,2,0,1:T(2,128)(2,1)S(1)}, bf16[64,4,2,64]{3,2,0,1:T(2,128)(2,1)}, u32[]{:S(2)}) copy-start(bf16[64,4,2,64]{3,2,0,1:T(2,128)(2,1)} %reshape.249) | copy-start | bytes 196612
  77.1 26.0 %collective-permute-start.4 = (f32[264,128]{1,0:T(8,128)S(1)}, f32[264,128]{1,0:T(8,128)S(1)}, u32[]{:S(2)}, u32[]{:S(2)}) collective-permute-start(f32[264,128]{1,0:T(8,128)S(1)} %pad_maximum_fusion.4), channel_id=1, source_target_pairs={{0,64},{4,68},{8,72},{12,76},{16,80},{20,84},{24,88},{28,92},{32,9... | collective-permute-start | bytes 405512 | tf_op jit(solution)/shard_map/ppermute | solution.py:58
  103.9 7.2 %collective-permute-start.5 = (f32[264,128]{1,0:T(8,128)S(1)}, f32[264,128]{1,0:T(8,128)S(1)}, u32[]{:S(2)}, u32[]{:S(2)}) collective-permute-start(f32[264,128]{1,0:T(8,128)S(1)} %pad_maximum_fusion.5), channel_id=1, source_target_pairs={{0,128},{4,132},{8,136},{12,140},{16,144},{20,148},{24,152},{28,15... | collective-permute-start | bytes 405512 | tf_op jit(solution)/shard_map/ppermute | solution.py:58
  111.9 8.4 %collective-permute-start.6 = (f32[264,128]{1,0:T(8,128)S(1)}, f32[264,128]{1,0:T(8,128)S(1)}, u32[]{:S(2)}, u32[]{:S(2)}) collective-permute-start(f32[264,128]{1,0:T(8,128)S(1)} %pad_maximum_fusion.6), channel_id=1, source_target_pairs={{0,256},{4,260},{8,264},{12,268},{16,272},{20,276},{24,280},{28,28... | collective-permute-start | bytes 405512 | tf_op jit(solution)/shard_map/ppermute | solution.py:58
  122.8 1.0 copy-start.5
  124.0 50.4 %copy-start.12 = (f32[1024]{0:T(1024)S(1)}, f32[1024]{0:T(1024)}, u32[]{:S(2)}) copy-start(f32[1024]{0:T(1024)} %param.29) | copy-start | bytes 12292
  124.0 24.8 %collective-permute-start.7 = (f32[64,4,1024]{2,0,1:T(8,128)S(1)}, f32[64,4,1024]{2,0,1:T(8,128)S(1)}, u32[]{:S(2)}, u32[]{:S(2)}) collective-permute-start(f32[64,4,1024]{2,0,1:T(8,128)S(1)} %fusion.28), channel_id=1, source_target_pairs={{0,1},{1,0},{2,3},{3,2},{4,5},{5,4},{6,7},{7,6},{8,9},{9,8},{10,11... | collective-permute-start | bytes 3145736 | tf_op jit(solution)/shard_map/ppermute | solution.py:154
  149.0 25.4 %collective-permute-start.8 = (f32[64,4,1024]{2,0,1:T(8,128)S(1)}, f32[64,4,1024]{2,0,1:T(8,128)S(1)}, u32[]{:S(2)}, u32[]{:S(2)}) collective-permute-start(f32[64,4,1024]{2,0,1:T(8,128)S(1)} %add.182), channel_id=1, source_target_pairs={{0,2},{1,3},{2,0},{3,1},{4,6},{5,7},{6,4},{7,5},{8,10},{9,11},{10,... | collective-permute-start | bytes 3145736 | tf_op jit(solution)/shard_map/ppermute | solution.py:154
  174.7 0.7 copy-start.9
  175.0 0.7 copy-start.8
  175.0 1.2 copy-start.15
  175.7 0.8 copy-start.18
  179.5 28.6 %copy-start.7 = (f32[1024]{0:T(1024)S(1)}, f32[1024]{0:T(1024)}, u32[]{:S(2)}) copy-start(f32[1024]{0:T(1024)} %param.35) | copy-start | bytes 12292
  208.1 1.1 copy-start.1
  208.1 1.4 copy-start.11
  209.4 0.7 copy-start.10
Sparse Core Ops, SparseCore 0:
  179.7 28.3 reduce-scatter.1
